TPU v7x, 128 devices: a whole 4x4x4 slice. The times are simulated.
128 devices in a mesh: shard: 8 (over y, core), tensor: 4 (over z), section: 4 (over x).
Axes of the slice: x: 4, y: 4, z: 4, core: 2. Of those that a mesh axis runs over, the one named last changes fastest.
Arguments:
- activations: bfloat16 [4, 16384, 2048], P('section', 'shard'), may hold values from -500 to 500, as said below
- out_grad: bfloat16 [4, 16384, 8192], P('section', 'shard', 'tensor'), may hold values from -30 to 30, as said below
- basis: float32 [4, 2048, 256], P('section', 'shard'), may hold values from -0.125 to 0.125
- first_moment: float32 [4, 256, 8192], P('section', 'shard', 'tensor'), may hold values from -6 to 6
- second_moment: float32 [4, 256, 8192], P('section', 'shard', 'tensor'), may hold values from 0.5 to 2
- gain_partial: float32 [4, 8, 2048], P('section', 'shard'), may hold values from -4096 to 4096
- gain_first: float32 [4, 2048], P('section', 'shard'), may hold values from -6 to 6
- gain_second: float32 [4, 2048], P('section', 'shard'), may hold values from 0.5 to 2
Outputs:
- update: float32 [4, 2048, 8192], P('section', 'shard', 'tensor')
- first_out: float32 [4, 256, 8192], P('section', 'shard', 'tensor')
- second_out: float32 [4, 256, 8192], P('section', 'shard', 'tensor')
- new_basis: float32 [4, 2048, 256], P('section', ('shard', 'tensor'))
- gain_step: float32 [4, 2048], P('section', 'shard')
- gain_first_out: float32 [4, 2048], P('section', 'shard')
- gain_second_out: float32 [4, 2048], P('section', 'shard')
Inputs may be any that keep to these rules, and one draw needn't show every extreme that they name: Real-valued activations whose column scales differ from column to column. `out_grad`: Real-valued gradients whose column scales differ from column to column.
All inputs are finite; a program needn't handle non-finite values.
Results may differ from a plain program's by a relative error of at most 0.0003.
Values sent between devices are 32-bit elements; how exact they have to be, the bound alone decides.
No kernel may reach another device: no remote copies, remote signals or barrier semaphores. Data moves between devices by JAX's collectives and lax.ppermute only.
A program may use at most 128 MiB of HBM per device.

v0:
```python
import jax
import jax.numpy as jnp
from jax import lax
from jax.sharding import PartitionSpec as P

D = 2048
FF = 8192
NS_STEPS = 5
STEP = 8


exact_mode = lax.Precision.HIGHEST
beta_one = 0.9
beta_two = 0.999
adam_eps = 1e-08
clip_eps = 1e-06
ns_eps = 1e-07
coef_first = 3.4445
coef_second = -4.775
coef_third = 2.0315
PAD = 8


def adam_direction(clipped, first_old, second_old):
    first_new = beta_one * first_old + (1.0 - beta_one) * clipped
    second_new = beta_two * second_old + (1.0 - beta_two) * clipped * clipped
    direction = (
        first_new
        / (1.0 - beta_one**STEP)
        / (jnp.sqrt(second_new / (1.0 - beta_two**STEP)) + adam_eps)
    )
    return (first_new, second_new, direction)


def mixer_of(current):
    gram = jnp.dot(current.T, current, precision=exact_mode)
    return coef_second * gram + coef_third * jnp.dot(gram, gram, precision=exact_mode)


def split3(x):
    hi = lax.reduce_precision(x, exponent_bits=8, mantissa_bits=7)
    rest = x - hi
    mid = lax.reduce_precision(rest, exponent_bits=8, mantissa_bits=7)
    lo = rest - mid
    return tuple(p.astype(jnp.bfloat16) for p in (hi, mid, lo))


def dot_split(lhs, rhs_pieces, dims):
    out = None
    for piece in rhs_pieces:
        term = lax.dot_general(lhs, piece, dims, preferred_element_type=jnp.float32)
        out = term if out is None else out + term
    return out


def butterfly_sum(x, axis):
    n = lax.axis_size(axis)
    k = 1
    while k < n:
        x = x + lax.ppermute(x, axis, [(i, i ^ k) for i in range(n)])
        k *= 2
    return x


def shards(
    activations, out_grad, basis, first_moment, second_moment, gain_partial, gain_first, gain_second
):
    tensors = lax.axis_size("tensor")
    shard_count = lax.axis_size("shard")
    shard_pos = lax.axis_index("shard")
    tensor_pos = lax.axis_index("tensor")
    layer_count = activations.shape[0]
    rows_here = basis.shape[1]
    rank_rows = first_moment.shape[1]
    cols_here = out_grad.shape[2]
    rank = basis.shape[2]
    out_rows = rows_here // tensors
    layer_index = 0
    tokens_in = activations[layer_index]
    grads_out = out_grad[layer_index]
    basis_here = basis[layer_index]

    partial_grad = lax.dot_general(
        tokens_in, grads_out, (((0,), (0,)), ((), ())), preferred_element_type=jnp.float32
    )
    grad_block = lax.psum_scatter(partial_grad, "shard", scatter_dimension=0, tiled=True)

    basis_full = lax.all_gather(basis_here, "shard", axis=0, tiled=True)
    token_basis = dot_split(tokens_in, split3(basis_full), (((1,), (0,)), ((), ())))
    part_proj = dot_split(grads_out, split3(token_basis), (((0,), (0,)), ((), ()))).T
    gain_row = gain_partial[layer_index, 0]
    gain_len = gain_row.shape[0]
    gain_rows = -(-gain_len // cols_here)
    gain_block = jnp.pad(gain_row, (0, gain_rows * cols_here - gain_len)).reshape(gain_rows, cols_here)
    extra = jnp.zeros((PAD - gain_rows % PAD, cols_here), jnp.float32)
    packed = butterfly_sum(jnp.concatenate([part_proj, gain_block, extra], axis=0), "shard")
    proj_full = packed[:rank]
    gain_total = packed[rank:rank + gain_rows].reshape(-1)[:gain_len]
    proj_rows = lax.dynamic_slice_in_dim(proj_full, shard_pos * rank_rows, rank_rows, 0)

    square_part = jnp.sum(grad_block * grad_block)
    refresh_part = lax.dot_general(
        grad_block, proj_full, (((1,), (1,)), ((), ())), precision=exact_mode
    )
    extra_r = jnp.zeros((PAD, rank), jnp.float32).at[0, 0].set(square_part)
    packed_r = butterfly_sum(jnp.concatenate([refresh_part, extra_r], axis=0), "tensor")
    gathered = lax.all_gather(packed_r, "shard", axis=0, tiled=False)
    refreshed = gathered[:, :rows_here].reshape(shard_count * rows_here, rank)
    square_st = jnp.sum(gathered[:, rows_here, 0])

    gain_own = lax.dynamic_slice_in_dim(gain_total, shard_pos * rows_here, rows_here, 0)
    square_local = square_st + jnp.sum(gain_total * gain_total)
    total_sq = lax.psum(square_local, "section")
    entry_count = float(lax.axis_size("section") * layer_count * (D * FF + D))
    clip = jnp.minimum(1.0, lax.rsqrt(total_sq / entry_count + clip_eps))

    first_new, second_new, direction = adam_direction(
        clip * proj_rows, first_moment[layer_index], second_moment[layer_index]
    )
    update_here = jnp.dot(
        basis_here, lax.all_gather(direction, "shard", axis=0, tiled=True), precision=exact_mode
    )

    current = refreshed / jnp.sqrt(jnp.sum(refreshed * refreshed) + ns_eps)
    for step_index in range(NS_STEPS - 1):
        current = coef_first * current + jnp.dot(current, mixer_of(current), precision=exact_mode)
    row_start = shard_pos * rows_here + tensor_pos * out_rows
    own = lax.dynamic_slice_in_dim(current, row_start, out_rows, 0)
    own = coef_first * own + jnp.dot(own, mixer_of(current), precision=exact_mode)

    gain_first_new, gain_second_new, gain_dir = adam_direction(
        clip * gain_own, gain_first[layer_index], gain_second[layer_index]
    )
    return (
        update_here[None],
        first_new[None],
        second_new[None],
        own[None],
        gain_dir[None],
        gain_first_new[None],
        gain_second_new[None],
    )


def solution(mesh):
    placed = (
        P("section", "shard", None),
        P("section", "shard", "tensor"),
        P("section", "shard", None),
        P("section", "shard", "tensor"),
        P("section", "shard", "tensor"),
        P("section", "shard", None),
        P("section", "shard"),
        P("section", "shard"),
    )
    return jax.shard_map(
        shards,
        mesh=mesh,
        in_specs=placed,
        out_specs=(
            P("section", "shard", "tensor"),
            P("section", "shard", "tensor"),
            P("section", "shard", "tensor"),
            P("section", ("shard", "tensor"), None),
            P("section", "shard"),
            P("section", "shard"),
            P("section", "shard"),
        ),
        check_vma=False,
    )
```

profile of v0, /device:TPU:1, one launch (start us, length us, event | category | flops | bytes accessed | tf_op | source)
XLA Modules:
  0.0 338.4 jit_solution(14491042343794681184)
XLA Ops:
  7.2 0.0 all-gather.8.cloned.1.call-start
  7.2 0.7 all-gather.8.cloned.1.call-update
  7.9 0.0 reduce-scatter.2.cloned.1.call-start
  7.9 24.3 %fusion.6 = f32[2048,2048]{1,0:T(8,128)} fusion(bf16[1,2048,2048]{2,1,0:T(8,128)(2,1)} %param.11, bf16[1,2048,2048]{2,1,0:T(8,128)(2,1)} %param.10), kind=kOutput, calls=%fused_computation.6 | convolution fusion | flops 17179869184 | bytes 33554432 | tf_op jit(solution)/shard_map/dot_general | solution.py:83
  32.2 0.0 reduce-scatter.2.cloned.1.call-update
  32.3 0.4 all-gather.10.cloned.1.call-start
  32.7 0.1 pad.10.clone
  32.8 5.9 %all-gather.8.cloned.1.call-done = f32[1,2048,256]{2,1,0:T(8,128)} async-done(((f32[1,256,256]{2,1,0:T(8,128)}), f32[1,2048,256]{2,1,0:T(8,128)}) %all-gather.8.cloned.1.call-update) | async-done | bytes 2097168 | tf_op jit(solution)/shard_map/all_gather | solution.py:88
  38.6 6.6 %fusion.12 = f32[2048,256]{1,0:T(8,128)S(1)} fusion(bf16[1,2048,2048]{2,1,0:T(8,128)(2,1)} %param.10, f32[1,2048,256]{2,1,0:T(8,128)} %all-gather.8.cloned.1.call-done), kind=kOutput, calls=%fused_computation.12 | convolution fusion | flops 2148532224 | bytes 12582912 | tf_op jit(solution)/shard_map/dot_general | solution.py:51
  45.2 0.0 slice-start.3
  45.3 6.1 %fusion.15 = f32[2048,256]{1,0:T(8,128)S(1)} fusion(bf16[1,2048,2048]{2,1,0:T(8,128)(2,1)} %param.10, f32[1,2048,256]{2,1,0:T(8,128)S(1)} %copy-done.7), kind=kOutput, calls=%fused_computation.23 | convolution fusion | flops 2150105088 | bytes 12582912 | tf_op jit(solution)/shard_map/dot_general | solution.py:51
  51.4 2.6 fusion.24
  54.0 2.4 fusion.2
  56.4 2.4 fusion
  58.8 15.1 %fusion.30 = f32[256,2048]{1,0:T(8,128)S(1)} fusion(f32[256,2048]{1,0:T(8,128)S(1)} %fusion, f32[256,2048]{1,0:T(8,128)S(1)} %fusion.2, bf16[1,2048,2048]{2,1,0:T(8,128)(2,1)S(1)} %bitcast.111, f32[2048,256]{1,0:T(8,128)S(1)} %fusion.24), kind=kOutput, calls=%fused_computation.33 | convolution fusion | flops 2149580800 | bytes 16777216 | tf_op jit(solution)/shard_map/dot_general | solution.py:51
  74.0 0.2 maximum_maximum_fusion
  74.2 0.4 collective-permute-start
  74.6 4.5 %collective-permute-done = f32[264,2048]{1,0:T(8,128)S(1)} collective-permute-done((f32[264,2048]{1,0:T(8,128)S(1)}, f32[264,2048]{1,0:T(8,128)S(1)}, u32[]{:S(2)}, u32[]{:S(2)}) %collective-permute-start) | collective-permute-done | bytes 2162720 | tf_op jit(solution)/shard_map/ppermute | solution.py:60
  79.1 0.3 fusion.53
  79.4 0.1 collective-permute-start.1
  79.5 72.0 %collective-permute-done.1 = f32[264,2048]{1,0:T(8,128)S(1)} collective-permute-done((f32[264,2048]{1,0:T(8,128)S(1)}, f32[264,2048]{1,0:T(8,128)S(1)}, u32[]{:S(2)}, u32[]{:S(2)}) %collective-permute-start.1) | collective-permute-done | bytes 2162720 | tf_op jit(solution)/shard_map/ppermute | solution.py:60
  151.5 0.4 add.122
  151.9 1.9 collective-permute-start.2
  153.8 70.2 %collective-permute-done.2 = f32[264,2048]{1,0:T(8,128)S(1)} collective-permute-done((f32[264,2048]{1,0:T(8,128)S(1)}, f32[264,2048]{1,0:T(8,128)S(1)}, u32[]{:S(2)}, u32[]{:S(2)}) %collective-permute-start.2) | collective-permute-done | bytes 2162720 | tf_op jit(solution)/shard_map/ppermute | solution.py:60
  224.0 0.3 add.123
  224.4 0.0 reduce-scatter.2.cloned.1.call-done
  224.4 2.9 multiply_reduce_fusion.1
  227.3 1.9 fusion.51
  229.2 0.7 select_maximum_fusion
  229.9 1.4 collective-permute-start.3
  231.2 5.7 %collective-permute-done.3 = f32[264,256]{1,0:T(8,128)S(1)} collective-permute-done((f32[264,256]{1,0:T(8,128)S(1)}, f32[264,256]{1,0:T(8,128)S(1)}, u32[]{:S(2)}, u32[]{:S(2)}) %collective-permute-start.3) | collective-permute-done | bytes 270368 | tf_op jit(solution)/shard_map/ppermute | solution.py:60
  236.9 0.7 fusion.50
  237.6 3.0 collective-permute-start.4
  240.6 4.8 %collective-permute-done.4 = f32[264,256]{1,0:T(8,128)S(1)} collective-permute-done((f32[264,256]{1,0:T(8,128)S(1)}, f32[264,256]{1,0:T(8,128)S(1)}, u32[]{:S(2)}, u32[]{:S(2)}) %collective-permute-start.4) | collective-permute-done | bytes 270368 | tf_op jit(solution)/shard_map/ppermute | solution.py:60
  245.3 0.8 add.125
  246.1 0.0 all-gather.10.cloned.1.call-update
  246.1 0.0 all-gather.6.cloned.1.call-start
  246.2 1.5 slice.32
  247.6 0.6 fusion.55
  248.2 27.3 %all-gather.10.cloned.1.call-done = f32[2112,256]{1,0:T(8,128)} async-done(((f32[264,256]{1,0:T(8,128)}), f32[2112,256]{1,0:T(8,128)}) %all-gather.10.cloned.1.call-update) | async-done | bytes 2162704 | tf_op jit(solution)/shard_map/all_gather | solution.py:107
  275.5 1.4 slice_reduce_fusion
  278.2 2.7 multiply_reduce_fusion
  280.9 8.9 %psum.7 = f32[]{:T(128)} all-reduce(f32[]{:T(128)S(6)} %add.126), channel_id=1, replica_groups=mesh['shard'=8,'tensor'=4,'section'=4] {'section'}, use_global_device_ids=true, to_apply=%region_4.5 | all-reduce | flops 1 | bytes 8 | tf_op jit(solution)/shard_map/psum | solution.py:113
  291.2 1.8 slice_divide_fusion
  293.1 3.5 %convolution_bitcast_fusion.1 = f32[256,256]{1,0:T(8,128)S(1)} fusion(f32[8,256,256]{2,1,0:T(8,128)S(1)} %slice_divide_fusion), kind=kOutput, calls=%fused_computation.50 | convolution fusion | flops 1610612736 | bytes 2359296 | tf_op jit(solution)/shard_map/dot_general | solution.py:36
  296.6 0.4 fusion.39
  297.0 2.0 fusion.47
  299.0 0.0 all-gather.6.cloned.1.call-update
  299.0 1.9 convolution_add_fusion.3
  300.9 3.6 %fusion.56 = f32[256,256]{1,0:T(8,128)S(1)} fusion(f32[2048,256]{1,0:T(8,128)S(1)} %convolution_add_fusion.3), kind=kOutput, calls=%fused_computation.77 | convolution fusion | flops 1610612736 | bytes 2359296 | tf_op jit(solution)/shard_map/dot_general | solution.py:36
  304.5 0.4 fusion.38
  304.9 1.9 convolution_add_fusion.2
  306.8 4.0 %fusion.57 = f32[256,256]{1,0:T(8,128)S(1)} fusion(f32[2048,256]{1,0:T(8,128)S(1)} %convolution_add_fusion.2), kind=kOutput, calls=%fused_computation.78 | convolution fusion | flops 1610612736 | bytes 2359296 | tf_op jit(solution)/shard_map/dot_general | solution.py:36
  310.9 0.4 fusion.37
  311.3 1.9 convolution_add_fusion.1
  313.2 3.6 %fusion.58 = f32[256,256]{1,0:T(8,128)S(1)} fusion(f32[2048,256]{1,0:T(8,128)S(1)} %convolution_add_fusion.1), kind=kOutput, calls=%fused_computation.79 | convolution fusion | flops 1610612736 | bytes 2359296 | tf_op jit(solution)/shard_map/dot_general | solution.py:36
  316.8 0.4 fusion.36
  317.2 1.9 convolution_add_fusion
  319.2 3.8 %fusion.59 = f32[256,256]{1,0:T(8,128)S(1)} fusion(f32[2048,256]{1,0:T(8,128)S(1)} %convolution_add_fusion), kind=kOutput, calls=%fused_computation.80 | convolution fusion | flops 1610612736 | bytes 2359296 | tf_op jit(solution)/shard_map/dot_general | solution.py:36
  323.0 0.4 fusion.35
  323.4 0.9 fusion.40
  324.3 0.6 add_divide_fusion.1
  324.9 5.0 %convolution_bitcast_fusion = f32[1,256,2048]{1,2,0:T(8,128)S(1)} fusion(f32[256,2048]{1,0:T(8,128)} %all-gather.6.cloned.1.call-done, f32[1,256,256]{2,1,0:T(8,128)S(1)} %copy-done.1), kind=kOutput, calls=%fused_computation.29 | convolution fusion | flops 1610612736 | bytes 4456448 | tf_op jit(solution)/shard_map/dot_general | solution.py:120
  329.9 1.8 copy.18
  (27 shorter events, 0.1 us)
Async XLA Ops:
  7.2 31.5 %all-gather.8.cloned.1.call-start = ((), (), s32[]{:S(2)}) async-start(), calls=%async_computation.3 | async-start | bytes 2359296 | tf_op jit(solution)/shard_map/all_gather | solution.py:88
  7.9 216.5 %reduce-scatter.2.cloned.1.call-start = ((), (), s32[]{:S(2)}) async-start(), calls=%async_computation.1 | async-start | bytes 18874368 | tf_op jit(solution)/shard_map/reduce_scatter | solution.py:86
  32.3 243.3 %all-gather.10.cloned.1.call-start = ((), (), s32[]{:S(2)}) async-start(), calls=%async_computation.4 | async-start | bytes 2433024 | tf_op jit(solution)/shard_map/all_gather | solution.py:107
  38.6 6.6 %copy-start.7 = (f32[1,2048,256]{2,1,0:T(8,128)S(1)}, f32[1,2048,256]{2,1,0:T(8,128)}, u32[]{:S(2)}) copy-start(f32[1,2048,256]{2,1,0:T(8,128)} %all-gather.8.cloned.1.call-done) | copy-start | bytes 6291460
  38.6 12.7 %slice-start.2 = ((s8[8388608]{0:T(1024)(128)(4,1)}), s8[4194304]{0:T(1024)(128)(4,1)S(1)}, s32[]{:S(2)}) async-start(s8[8388608]{0:T(1024)(128)(4,1)} %bitcast.118), calls=%async_computation.7 | async-start | bytes 8388608
  38.6 15.4 %slice-start = ((s8[8388608]{0:T(1024)(128)(4,1)}), s8[4194304]{0:T(1024)(128)(4,1)S(1)}, s32[]{:S(2)}) async-start(s8[8388608]{0:T(1024)(128)(4,1)} %bitcast.110), calls=%async_computation.5 | async-start | bytes 8388608
  45.2 6.1 %slice-start.3 = ((s8[8388608]{0:T(1024)(128)(4,1)}), s8[4194304]{0:T(1024)(128)(4,1)S(1)}, s32[]{:S(2)}) async-start(s8[8388608]{0:T(1024)(128)(4,1)} %bitcast.118), calls=%async_computation.8 | async-start | bytes 8388608
  45.3 8.7 %slice-start.1 = ((s8[8388608]{0:T(1024)(128)(4,1)}), s8[4194304]{0:T(1024)(128)(4,1)S(1)}, s32[]{:S(2)}) async-start(s8[8388608]{0:T(1024)(128)(4,1)} %bitcast.110), calls=%async_computation.6 | async-start | bytes 8388608
  58.8 15.2 %copy-start.4 = (f32[1,1,2048]{2,1,0:T(1,128)S(1)}, f32[1,1,2048]{2,1,0:T(1,128)}, u32[]{:S(2)}) copy-start(f32[1,1,2048]{2,1,0:T(1,128)} %param.15) | copy-start | bytes 24580
  74.2 4.9 %collective-permute-start = (f32[264,2048]{1,0:T(8,128)S(1)}, f32[264,2048]{1,0:T(8,128)S(1)}, u32[]{:S(2)}, u32[]{:S(2)}) collective-permute-start(f32[264,2048]{1,0:T(8,128)S(1)} %maximum_maximum_fusion), channel_id=1, source_target_pairs={{0,16},{16,0},{32,48},{48,32},{64,80},{80,64},{96,112},{112,96},{1... | collective-permute-start | bytes 6488072 | tf_op jit(solution)/shard_map/ppermute | solution.py:60
  79.4 72.1 %collective-permute-start.1 = (f32[264,2048]{1,0:T(8,128)S(1)}, f32[264,2048]{1,0:T(8,128)S(1)}, u32[]{:S(2)}, u32[]{:S(2)}) collective-permute-start(f32[264,2048]{1,0:T(8,128)S(1)} %fusion.53), channel_id=1, source_target_pairs={{0,32},{16,48},{32,0},{48,16},{64,96},{80,112},{96,64},{112,80},{1... | collective-permute-start | bytes 6488072 | tf_op jit(solution)/shard_map/ppermute | solution.py:60
  151.9 72.2 %collective-permute-start.2 = (f32[264,2048]{1,0:T(8,128)S(1)}, f32[264,2048]{1,0:T(8,128)S(1)}, u32[]{:S(2)}, u32[]{:S(2)}) collective-permute-start(f32[264,2048]{1,0:T(8,128)S(1)} %add.122), channel_id=1, source_target_pairs={{0,64},{16,80},{32,96},{48,112},{64,0},{80,16},{96,32},{112,48},{1... | collective-permute-start | bytes 6488072 | tf_op jit(solution)/shard_map/ppermute | solution.py:60
  224.4 2.9 copy-start
  229.9 7.1 %collective-permute-start.3 = (f32[264,256]{1,0:T(8,128)S(1)}, f32[264,256]{1,0:T(8,128)S(1)}, u32[]{:S(2)}, u32[]{:S(2)}) collective-permute-start(f32[264,256]{1,0:T(8,128)S(1)} %select_maximum_fusion), channel_id=1, source_target_pairs={{0,4},{4,0},{8,12},{12,8},{1,5},{5,1},{9,13},{13,9},{2,6},{6,2},{1... | collective-permute-start | bytes 811016 | tf_op jit(solution)/shard_map/ppermute | solution.py:60
  237.6 7.7 %collective-permute-start.4 = (f32[264,256]{1,0:T(8,128)S(1)}, f32[264,256]{1,0:T(8,128)S(1)}, u32[]{:S(2)}, u32[]{:S(2)}) collective-permute-start(f32[264,256]{1,0:T(8,128)S(1)} %fusion.50), channel_id=1, source_target_pairs={{0,8},{4,12},{8,0},{12,4},{1,9},{5,13},{9,1},{13,5},{2,10},{6,14},... | collective-permute-start | bytes 811016 | tf_op jit(solution)/shard_map/ppermute | solution.py:60
  246.1 78.7 %all-gather.6.cloned.1.call-start = ((), (), s32[]{:S(2)}) async-start(), calls=%async_computation.2 | async-start | bytes 2359296 | tf_op jit(solution)/shard_map/all_gather | solution.py:121
  293.0 3.9 %copy-start.2 = (f32[1,32,2048]{2,1,0:T(8,128)S(1)}, f32[1,32,2048]{2,1,0:T(8,128)}, u32[]{:S(2)}) copy-start(f32[1,32,2048]{2,1,0:T(8,128)} %param.14) | copy-start | bytes 786436
  293.1 3.9 %copy-start.3 = (f32[1,32,2048]{2,1,0:T(8,128)S(1)}, f32[1,32,2048]{2,1,0:T(8,128)}, u32[]{:S(2)}) copy-start(f32[1,32,2048]{2,1,0:T(8,128)} %param.13) | copy-start | bytes 786436
  319.1 5.1 %copy-start.5 = (f32[1,256]{1,0:T(1,128)S(1)}, f32[1,256]{1,0:T(1,128)}, u32[]{:S(2)}) copy-start(f32[1,256]{1,0:T(1,128)} %param.16) | copy-start | bytes 3076
  319.1 5.1 %copy-start.6 = (f32[1,256]{1,0:T(1,128)S(1)}, f32[1,256]{1,0:T(1,128)}, u32[]{:S(2)}) copy-start(f32[1,256]{1,0:T(1,128)} %param.17) | copy-start | bytes 3076
  319.1 5.7 %copy-start.1 = (f32[1,256,256]{2,1,0:T(8,128)S(1)}, f32[1,256,256]{2,1,0:T(8,128)}, u32[]{:S(2)}) copy-start(f32[1,256,256]{2,1,0:T(8,128)} %param.12) | copy-start | bytes 786436
Sparse Core Ops, SparseCore 0:
  9.7 28.8 all-gather.7
  41.1 181.5 reduce-scatter.1
  246.2 29.2 all-gather.9
  299.1 25.5 all-gather.5
where the time goes:
time: 343 us; the launch traced here: 338 us
  waiting for transfers between devices  191 us (56%)
  matrix products  95.4 us (28%)
  between operations  17 us (5%)
  other arithmetic  15.3 us (4%)
  blocking collectives  8.88 us (3%)
  starting transfers between devices  7.26 us (2%)
    ppermute x5, waiting for transfers between devices, butterfly_sum(): x = x + lax.ppermute(x, axis, [(i, i ^ k) for i in range(n)])  157 us
    dot_general x6, matrix products, dot_split(): term = lax.dot_general(lhs, piece, dims, preferred_element_type=jnp.float32)  35.2 us
    all_gather x1, waiting for transfers between devices, shards(): gathered = lax.all_gather(packed_r, 'shard', axis=0, tiled=False)  27.3 us
    dot_general x1, matrix products, shards(): lax.dot_general(tokens_in, grads_out, (((0,), (0,)), ((), ())), preferred...  24.3 us
    dot_general x5, matrix products, mixer_of(): gram = jnp.dot(current.T, current, precision=exact_mode)  18.6 us
    psum x1, blocking collectives, shards(): total_sq = lax.psum(square_local, 'section')  8.88 us
    dot_general x4, matrix products, shards(): jnp.dot(current, mixer_of(current), precision=exact_mode)  7.6 us
  transfers between devices with their start and end apart: 9, of which 7 were waited for; matrix products, arithmetic and copies ran while one was open for 26% of the time, Pallas kernels for 0%

commit v1 on v0

--- a/solution.py
+++ b/solution.py
@@ -84,16 +84,13 @@
         tokens_in, grads_out, (((0,), (0,)), ((), ())), preferred_element_type=jnp.float32
     )
     grad_block = lax.psum_scatter(partial_grad, "shard", scatter_dimension=0, tiled=True)
-
-    basis_full = lax.all_gather(basis_here, "shard", axis=0, tiled=True)
-    token_basis = dot_split(tokens_in, split3(basis_full), (((1,), (0,)), ((), ())))
-    part_proj = dot_split(grads_out, split3(token_basis), (((0,), (0,)), ((), ()))).T
+    part_proj = jnp.dot(basis_here.T, grad_block, precision=exact_mode)
     gain_row = gain_partial[layer_index, 0]
     gain_len = gain_row.shape[0]
     gain_rows = -(-gain_len // cols_here)
     gain_block = jnp.pad(gain_row, (0, gain_rows * cols_here - gain_len)).reshape(gain_rows, cols_here)
     extra = jnp.zeros((PAD - gain_rows % PAD, cols_here), jnp.float32)
-    packed = butterfly_sum(jnp.concatenate([part_proj, gain_block, extra], axis=0), "shard")
+    packed = lax.psum(jnp.concatenate([part_proj, gain_block, extra], axis=0), "shard")
     proj_full = packed[:rank]
     gain_total = packed[rank:rank + gain_rows].reshape(-1)[:gain_len]
     proj_rows = lax.dynamic_slice_in_dim(proj_full, shard_pos * rank_rows, rank_rows, 0)

time: 343 us -> 323 us (0.942)
  matrix products: 95.4 us -> 73.9 us
  waiting for transfers between devices: 191 us -> 195 us
    ppermute x5 -> x2, waiting for transfers between devices: 157 us -> 8.68 us  [butterfly_sum(): x = x + lax.ppermute(x, axis, [(i, i ^ k) for i in range(n)])]
    reduce_scatter x1, waiting for transfers between devices: 0.02 us -> 94.5 us  [shards(): lax.psum_scatter(partial_grad, 'shard', scatter_dimension=0, tiled=True)]
    psum x0 -> x1, waiting for transfers between devices: none -> 61.7 us  [shards(): lax.psum(jnp.concatenate([part_proj, gain_block, extra], axis=0), 'shard')]
    dot_general x6 -> x1, matrix products: 35.2 us -> 3.63 us  [shards(): part_proj = jnp.dot(basis_here.T, grad_block, precision=exact_mode)]
    dot_general x4, matrix products: 7.6 us -> 16.4 us  [shards(): jnp.dot(current, mixer_of(current), precision=exact_mode)]
    all_gather x1 -> x0, waiting for transfers between devices: 5.86 us -> none  [shards(): basis_full = lax.all_gather(basis_here, 'shard', axis=0, tiled=True)]
  transfers between devices with their start and end apart: 9 -> 6, of which waited for: 7 -> 5; matrix products, arithmetic and copies ran while one was open for 26% -> 12% of each run, Pallas kernels for 0% -> 0%
where the time goes in v1:
time: 323 us; the launch traced here: 319 us
  waiting for transfers between devices  195 us (60%)
  matrix products  73.9 us (23%)
  between operations  16.9 us (5%)
  other arithmetic  14.1 us (4%)
  blocking collectives  8.91 us (3%)
  local copies, waits for them, and re-layouts  4.91 us (2%)
  starting transfers between devices  4.72 us (1%)
    reduce_scatter x1, waiting for transfers between devices, shards(): lax.psum_scatter(partial_grad, 'shard', scatter_dimension=0, tiled=True)  94.5 us
    psum x1, waiting for transfers between devices, shards(): lax.psum(jnp.concatenate([part_proj, gain_block, extra], axis=0), 'shard')  61.7 us
    all_gather x1, waiting for transfers between devices, shards(): gathered = lax.all_gather(packed_r, 'shard', axis=0, tiled=False)  30.2 us
    dot_general x1, matrix products, shards(): lax.dot_general(tokens_in, grads_out, (((0,), (0,)), ((), ())), preferred...  24.4 us
    dot_general x5, matrix products, mixer_of(): gram = jnp.dot(current.T, current, precision=exact_mode)  18.1 us
    dot_general x4, matrix products, shards(): jnp.dot(current, mixer_of(current), precision=exact_mode)  16.4 us
    psum x1, blocking collectives, shards(): total_sq = lax.psum(square_local, 'section')  8.91 us
    ppermute x2, waiting for transfers between devices, butterfly_sum(): x = x + lax.ppermute(x, axis, [(i, i ^ k) for i in range(n)])  8.68 us
  transfers between devices with their start and end apart: 6, of which 5 were waited for; matrix products, arithmetic and copies ran while one was open for 12% of the time, Pallas kernels for 0%

profile of v1, /device:TPU:1, one launch (start us, length us, event | category | flops | bytes accessed | tf_op | source)
XLA Modules:
  0.0 318.5 jit_solution(17993326626726536140)
XLA Ops:
  7.2 0.0 copy-start
  7.2 0.0 reduce-scatter.2.cloned.1.call-start
  7.2 24.4 %fusion = f32[2048,2048]{1,0:T(8,128)} fusion(bf16[1,2048,2048]{2,1,0:T(8,128)(2,1)} %param.11, bf16[1,2048,2048]{2,1,0:T(8,128)(2,1)} %param.10), kind=kOutput, calls=%fused_computation | convolution fusion | flops 17179869184 | bytes 33554432 | tf_op jit(solution)/shard_map/dot_general | solution.py:83
  31.6 0.0 reduce-scatter.2.cloned.1.call-update
  31.6 0.0 all-reduce.3.cloned.1.call-start
  31.7 0.1 pad.10.clone
  31.8 0.0 copy-start.5
  31.8 94.5 %reduce-scatter.2.cloned.1.call-done = f32[256,2048]{1,0:T(8,128)} async-done(((f32[2048,2048]{1,0:T(8,128)}), f32[256,2048]{1,0:T(8,128)}) %reduce-scatter.2.cloned.1.call-update) | async-done | bytes 2097168 | tf_op jit(solution)/shard_map/reduce_scatter | solution.py:86
  126.2 0.0 copy-done
  126.2 3.6 %convolution_bitcast_fusion.1 = f32[256,2048]{1,0:T(8,128)S(1)} fusion(f32[256,2048]{1,0:T(8,128)} %reduce-scatter.2.cloned.1.call-done, f32[1,256,256]{2,1,0:T(8,128)S(1)} %copy-done), kind=kOutput, calls=%fused_computation.8 | convolution fusion | flops 1610612736 | bytes 4456448 | tf_op jit(solution)/shard_map/dot_general | solution.py:87
  129.9 0.0 copy-done.5
  129.9 1.5 maximum_maximum_fusion
  131.4 0.0 all-reduce.3.cloned.1.call-update
  131.5 0.0 all-gather.6.cloned.1.call-start
  131.5 1.5 copy-done.1
  133.0 1.1 multiply_reduce_fusion.1
  134.2 61.7 %all-reduce.3.cloned.1.call-done = f32[264,2048]{1,0:T(8,128)} async-done(((f32[264,2048]{1,0:T(8,128)}), f32[264,2048]{1,0:T(8,128)}) %all-reduce.3.cloned.1.call-update) | async-done | bytes 2162704 | tf_op jit(solution)/shard_map/psum | solution.py:93
  195.9 3.5 %fusion.18 = f32[256,256]{1,0:T(8,128)S(1)} fusion(f32[256,2048]{1,0:T(8,128)S(1)} %copy-done.1, f32[264,2048]{1,0:T(8,128)} %all-reduce.3.cloned.1.call-done), kind=kOutput, calls=%fused_computation.47 | convolution fusion | flops 1610612736 | bytes 4456448 | tf_op jit(solution)/shard_map/dot_general | solution.py:99
  199.3 0.0 copy-start.2
  199.3 0.8 select_maximum_fusion
  200.2 1.4 collective-permute-start
  201.5 4.0 %collective-permute-done = f32[264,256]{1,0:T(8,128)S(1)} collective-permute-done((f32[264,256]{1,0:T(8,128)S(1)}, f32[264,256]{1,0:T(8,128)S(1)}, u32[]{:S(2)}, u32[]{:S(2)}) %collective-permute-start) | collective-permute-done | bytes 270368 | tf_op jit(solution)/shard_map/ppermute | solution.py:60
  205.5 0.7 fusion.17
  206.2 2.9 collective-permute-start.1
  209.2 4.6 %collective-permute-done.1 = f32[264,256]{1,0:T(8,128)S(1)} collective-permute-done((f32[264,256]{1,0:T(8,128)S(1)}, f32[264,256]{1,0:T(8,128)S(1)}, u32[]{:S(2)}, u32[]{:S(2)}) %collective-permute-start.1) | collective-permute-done | bytes 270368 | tf_op jit(solution)/shard_map/ppermute | solution.py:60
  213.8 0.7 add.97
  214.6 0.0 all-gather.6.cloned.1.call-update
  214.6 0.3 all-gather.4.cloned.1.call-start
  214.9 0.0 copy-done.2
  214.9 1.5 slice.32
  216.4 0.6 fusion.21
  217.0 30.2 %all-gather.6.cloned.1.call-done = f32[2112,256]{1,0:T(8,128)} async-done(((f32[264,256]{1,0:T(8,128)}), f32[2112,256]{1,0:T(8,128)}) %all-gather.6.cloned.1.call-update) | async-done | bytes 2162704 | tf_op jit(solution)/shard_map/all_gather | solution.py:104
  247.2 2.7 multiply_reduce_fusion
  249.9 1.4 slice_reduce_fusion
  252.0 1.8 slice_divide_fusion
  253.8 0.0 copy-start.3
  253.8 0.0 copy-start.4
  253.8 3.5 %convolution_bitcast_fusion.2 = f32[256,256]{1,0:T(8,128)S(1)} fusion(f32[8,256,256]{2,1,0:T(8,128)S(1)} %slice_divide_fusion), kind=kOutput, calls=%fused_computation.23 | convolution fusion | flops 1610612736 | bytes 2359296 | tf_op jit(solution)/shard_map/dot_general | solution.py:36
  258.6 0.4 fusion.7
  259.0 8.9 %psum.15 = f32[]{:T(128)} all-reduce(f32[]{:T(128)S(6)} %add.98), channel_id=1, replica_groups=mesh['shard'=8,'tensor'=4,'section'=4] {'section'}, use_global_device_ids=true, to_apply=%region_5.6 | all-reduce | flops 1 | bytes 8 | tf_op jit(solution)/shard_map/psum | solution.py:110
  268.6 0.0 copy-done.3
  268.6 0.0 copy-done.4
  268.6 2.0 fusion.14
  270.6 0.0 all-gather.4.cloned.1.call-update
  270.7 1.9 convolution_add_fusion.3
  272.6 3.6 %fusion.22 = f32[256,256]{1,0:T(8,128)S(1)} fusion(f32[2048,256]{1,0:T(8,128)S(1)} %convolution_add_fusion.3), kind=kOutput, calls=%fused_computation.50 | convolution fusion | flops 1610612736 | bytes 2359296 | tf_op jit(solution)/shard_map/dot_general | solution.py:36
  276.2 0.4 fusion.6
  276.6 1.9 convolution_add_fusion.2
  278.5 3.6 %fusion.23 = f32[256,256]{1,0:T(8,128)S(1)} fusion(f32[2048,256]{1,0:T(8,128)S(1)} %convolution_add_fusion.2), kind=kOutput, calls=%fused_computation.51 | convolution fusion | flops 1610612736 | bytes 2359296 | tf_op jit(solution)/shard_map/dot_general | solution.py:36
  282.2 0.4 fusion.5
  282.5 10.7 %convolution_add_fusion.1 = f32[2048,256]{1,0:T(8,128)S(1)} fusion(f32[2048,256]{1,0:T(8,128)S(1)} %convolution_add_fusion.2, f32[256,256]{1,0:T(8,128)S(1)} %fusion.5), kind=kOutput, calls=%fused_computation.4 | convolution fusion | flops 1611661312 | bytes 4456448 | tf_op jit(solution)/shard_map/dot_general | solution.py:123
  293.2 3.6 %fusion.24 = f32[256,256]{1,0:T(8,128)S(1)} fusion(f32[2048,256]{1,0:T(8,128)S(1)} %convolution_add_fusion.1), kind=kOutput, calls=%fused_computation.52 | convolution fusion | flops 1610612736 | bytes 2359296 | tf_op jit(solution)/shard_map/dot_general | solution.py:36
  296.9 0.4 fusion.4
  297.3 1.9 convolution_add_fusion
  299.2 0.0 copy-start.6
  299.2 0.0 copy-start.7
  299.2 3.6 %fusion.25 = f32[256,256]{1,0:T(8,128)S(1)} fusion(f32[2048,256]{1,0:T(8,128)S(1)} %convolution_add_fusion), kind=kOutput, calls=%fused_computation.53 | convolution fusion | flops 1610612736 | bytes 2359296 | tf_op jit(solution)/shard_map/dot_general | solution.py:36
  302.8 0.4 fusion.3
  303.2 0.9 fusion.8
  304.1 0.0 copy-done.6
  304.1 0.0 copy-done.7
  304.1 0.6 add_divide_fusion.1
  304.7 5.2 %convolution_bitcast_fusion = f32[1,256,2048]{1,2,0:T(8,128)S(1)} fusion(f32[256,2048]{1,0:T(8,128)} %all-gather.4.cloned.1.call-done, f32[1,256,256]{2,1,0:T(8,128)S(1)} %copy-done), kind=kOutput, calls=%fused_computation.7 | convolution fusion | flops 1610612736 | bytes 4456448 | tf_op jit(solution)/shard_map/dot_general | solution.py:117
  310.0 1.8 copy.16
  (3 shorter events, 0.0 us)
Async XLA Ops:
  7.2 119.1 %copy-start = (f32[1,256,256]{2,1,0:T(8,128)S(1)}, f32[1,256,256]{2,1,0:T(8,128)}, u32[]{:S(2)}) copy-start(f32[1,256,256]{2,1,0:T(8,128)} %param.12) | copy-start | bytes 786436
  7.2 119.1 %reduce-scatter.2.cloned.1.call-start = ((), (), s32[]{:S(2)}) async-start(), calls=%async_computation.1 | async-start | bytes 18874368 | tf_op jit(solution)/shard_map/reduce_scatter | solution.py:86
  31.6 164.2 %all-reduce.3.cloned.1.call-start = ((), (), s32[]{:S(2)}) async-start(), calls=%async_computation.2 | async-start | bytes 4325376 | tf_op jit(solution)/shard_map/psum | solution.py:93
  31.8 98.1 %copy-start.5 = (f32[1,1,2048]{2,1,0:T(1,128)S(1)}, f32[1,1,2048]{2,1,0:T(1,128)}, u32[]{:S(2)}) copy-start(f32[1,1,2048]{2,1,0:T(1,128)} %param.15) | copy-start | bytes 24580
  131.4 1.6 copy-start.1
  131.5 115.7 %all-gather.6.cloned.1.call-start = ((), (), s32[]{:S(2)}) async-start(), calls=%async_computation.4 | async-start | bytes 2433024 | tf_op jit(solution)/shard_map/all_gather | solution.py:104
  199.3 15.6 %copy-start.2 = (f32[264,2048]{1,0:T(8,128)S(1)}, f32[264,2048]{1,0:T(8,128)}, u32[]{:S(2)}) copy-start(f32[264,2048]{1,0:T(8,128)} %all-reduce.3.cloned.1.call-done) | copy-start | bytes 6488068
  200.2 5.4 %collective-permute-start = (f32[264,256]{1,0:T(8,128)S(1)}, f32[264,256]{1,0:T(8,128)S(1)}, u32[]{:S(2)}, u32[]{:S(2)}) collective-permute-start(f32[264,256]{1,0:T(8,128)S(1)} %select_maximum_fusion), channel_id=1, source_target_pairs={{0,4},{4,0},{8,12},{12,8},{1,5},{5,1},{9,13},{13,9},{2,6},{6,2},{1... | collective-permute-start | bytes 811016 | tf_op jit(solution)/shard_map/ppermute | solution.py:60
  206.2 7.6 %collective-permute-start.1 = (f32[264,256]{1,0:T(8,128)S(1)}, f32[264,256]{1,0:T(8,128)S(1)}, u32[]{:S(2)}, u32[]{:S(2)}) collective-permute-start(f32[264,256]{1,0:T(8,128)S(1)} %fusion.17), channel_id=1, source_target_pairs={{0,8},{4,12},{8,0},{12,4},{1,9},{5,13},{9,1},{13,5},{2,10},{6,14},... | collective-permute-start | bytes 811016 | tf_op jit(solution)/shard_map/ppermute | solution.py:60
  214.6 90.1 %all-gather.4.cloned.1.call-start = ((), (), s32[]{:S(2)}) async-start(), calls=%async_computation.3 | async-start | bytes 2359296 | tf_op jit(solution)/shard_map/all_gather | solution.py:118
  253.8 14.8 %copy-start.3 = (f32[1,32,2048]{2,1,0:T(8,128)S(1)}, f32[1,32,2048]{2,1,0:T(8,128)}, u32[]{:S(2)}) copy-start(f32[1,32,2048]{2,1,0:T(8,128)} %param.14) | copy-start | bytes 786436
  253.8 14.8 %copy-start.4 = (f32[1,32,2048]{2,1,0:T(8,128)S(1)}, f32[1,32,2048]{2,1,0:T(8,128)}, u32[]{:S(2)}) copy-start(f32[1,32,2048]{2,1,0:T(8,128)} %param.13) | copy-start | bytes 786436
  299.2 5.0 %copy-start.6 = (f32[1,256]{1,0:T(1,128)S(1)}, f32[1,256]{1,0:T(1,128)}, u32[]{:S(2)}) copy-start(f32[1,256]{1,0:T(1,128)} %param.16) | copy-start | bytes 3076
  299.2 4.9 %copy-start.7 = (f32[1,256]{1,0:T(1,128)S(1)}, f32[1,256]{1,0:T(1,128)}, u32[]{:S(2)}) copy-start(f32[1,256]{1,0:T(1,128)} %param.17) | copy-start | bytes 3076
Sparse Core Ops, SparseCore 0:
  31.8 94.4 reduce-scatter.1
  131.6 64.2 all-reduce.2
  214.7 32.4 all-gather.5
  270.8 25.5 all-gather.3
